TPU v7x, 32 devices: a whole 2x2x4 slice. The times are simulated.
32 devices in a mesh: atoms: 8 (over y, x, core), bands: 4 (over z).
Axes of the slice: x: 2, y: 2, z: 4, core: 2. Of those that a mesh axis runs over, the one named last changes fastest.
Arguments:
- subspace: bfloat16 [512, 6144], P('bands', 'atoms'), may hold values from -120 to 120
- diag_block: bfloat16 [6144, 768], P('atoms'), may hold values from -0.0625 to 0.0625
- pair_block: bfloat16 [2, 6144, 768], P(None, 'atoms'), may hold values from -0.0625 to 0.0625
- pair_pattern: int32 [2, 32, 4], P(None, 'atoms'), may hold values 0 or 1
- atom_sizes: int32 [8, 4], replicated, may hold values from 1 to 256, 768 in all within a row
- rotations: bfloat16 [4, 512, 512], P(None, None, 'bands'), may hold values from -0.25 to 0.25
Outputs:
- rotated: float32 [512, 6144], P('bands', 'atoms')
Inputs may be any that keep to these rules, and one draw needn't show every extreme that they name: `atom_sizes`: each row holds the orbital counts of the 4 atoms of one partition in order and sums to 768.
All inputs are finite; a program needn't handle non-finite values. No bound on the sum of `pair_pattern` on one device may be relied on, other than what follows from the above.
Results may differ from a plain program's by a relative error of at most 0.028.
Values may be sent and summed in bfloat16 or wider, within the bound.
No kernel may reach another device: no remote copies, remote signals or barrier semaphores. Data moves between devices by JAX's collectives and lax.ppermute only.
A program may use at most 64 MiB of HBM per device.

v0:
```python
import jax
import jax.numpy as jnp
from jax import lax
from jax.sharding import PartitionSpec as P

ROUNDS = 2
DEGREE = 8
ROTS = 4
filter_center = 0.1
filter_half = 1.25
norm_eps = 1e-06


def swapped(value, axis, stride):
    mask = 2**stride
    pairs = [(source, source ^ mask) for source in range(lax.axis_size(axis))]
    return lax.ppermute(value, axis, pairs)


def atom_onehot(atom_counts, length_total):
    atom_ends = jnp.cumsum(atom_counts, axis=-1)
    atom_starts = atom_ends - atom_counts
    positions = jnp.arange(length_total, dtype=jnp.int32)
    inside = (positions >= atom_starts[..., None]) & (positions < atom_ends[..., None])
    return inside.astype(jnp.float32)


def diagonal_weights(onehot_rows):
    levels = jnp.arange(onehot_rows.shape[0], dtype=jnp.float32)
    atom_index = jnp.sum(onehot_rows * levels[:, None], axis=0)
    upper_flag = (atom_index[:, None] < atom_index[None, :]).astype(jnp.float32)
    same_atom = (atom_index[:, None] == atom_index[None, :]).astype(jnp.float32)
    return upper_flag + 0.5 * same_atom


def apply_operator(values, diag_sym, coupling):
    result = jnp.dot(values, diag_sym, preferred_element_type=jnp.float32)
    for round_index in range(ROUNDS):
        pair_mat = coupling[round_index]
        other_rows = swapped(values, "atoms", round_index)
        own_term = lax.dot_general(
            other_rows, pair_mat, (((1,), (1,)), ((), ())), preferred_element_type=jnp.float32
        )
        sent_term = jnp.dot(values, pair_mat, preferred_element_type=jnp.float32)
        returned = swapped(sent_term.astype(jnp.bfloat16), "atoms", round_index).astype(
            sent_term.dtype
        )
        result = result + own_term + returned
    return result


def body(subspace, diag_block, pair_block, pair_pattern, atom_sizes, rotations):
    orb_dev = diag_block.shape[1]
    atoms_here = lax.axis_index("atoms")
    onehot_own = atom_onehot(
        lax.dynamic_index_in_dim(atom_sizes, atoms_here, 0, keepdims=False), orb_dev
    )
    upper_part = diag_block.astype(jnp.float32) * diagonal_weights(onehot_own)
    diag_sym = (upper_part + upper_part.T).astype(jnp.bfloat16)
    coupling = []
    for round_index in range(ROUNDS):
        partner = jnp.bitwise_xor(atoms_here, 1 << round_index)
        onehot_other = atom_onehot(
            lax.dynamic_index_in_dim(atom_sizes, partner, 0, keepdims=False), orb_dev
        )
        pattern = pair_pattern[round_index].astype(jnp.float32)
        right_side = jnp.dot(pattern, onehot_other, precision=lax.Precision.HIGHEST)
        pair_mask = lax.dot_general(
            onehot_own, right_side, (((0,), (0,)), ((), ())), precision=lax.Precision.HIGHEST
        )
        pair_mat = (pair_block[round_index].astype(jnp.float32) * pair_mask).astype(jnp.bfloat16)
        coupling.append(pair_mat)
    previous = subspace.astype(jnp.float32)
    current = (
        apply_operator(subspace, diag_sym, coupling) - filter_center * previous
    ) / filter_half
    for degree_index in range(1, DEGREE):
        applied = apply_operator(current.astype(jnp.bfloat16), diag_sym, coupling)
        following = 2.0 * (applied - filter_center * current) / filter_half - previous
        previous, current = (current, following)
    total_orbitals = orb_dev * lax.axis_size("atoms")
    basis_rows = current
    for rotation_index in range(ROTS):
        rounded = basis_rows.astype(jnp.bfloat16)
        local_cols = rotations[rotation_index]
        mixed_rows = lax.dot_general(
            local_cols,
            lax.all_gather(rounded, "bands", axis=0, tiled=True),
            (((0,), (0,)), ((), ())),
            preferred_element_type=jnp.float32,
        )
        squares = lax.psum(jnp.sum(mixed_rows * mixed_rows, axis=1), "atoms")
        col_norm = jnp.sqrt(squares / total_orbitals + norm_eps)
        basis_rows = mixed_rows / col_norm[:, None]
    return basis_rows


def solution(mesh):
    placed = (
        P("bands", "atoms"),
        P("atoms", None),
        P(None, "atoms", None),
        P(None, "atoms", None),
        P(),
        P(None, None, "bands"),
    )
    return jax.shard_map(
        body, mesh=mesh, in_specs=placed, out_specs=P("bands", "atoms"), check_vma=False
    )
```

profile of v0, /device:TPU:0, one launch (start us, length us, event | category | flops | bytes accessed | tf_op | source)
XLA Modules:
  0.0 228.8 jit_solution(13515440379078869902)
XLA Ops:
  0.0 2.9 %collective-permute-start.2 = (bf16[128,768]{1,0:T(8,128)(2,1)}, bf16[128,768]{1,0:T(8,128)(2,1)}, u32[]{:S(2)}, u32[]{:S(2)}) collective-permute-start(bf16[128,768]{1,0:T(8,128)(2,1)} %param.6), channel_id=1, source_target_pairs={{0,8},{4,12},{8,0},{12,4},{16,24},{20,28},{24,16},{28,20},{1,9},{5... | collective-permute-start | bytes 589832 | tf_op jit(solution)/shard_map/ppermute | solution.py:17
  5.7 2.7 %fusion.1 = bf16[768,768]{1,0:T(8,128)(2,1)S(1)} fusion(f32[768,4]{1,0:T(8,128)S(1)} %fusion.77, bf16[2,768,768]{2,1,0:T(8,128)(2,1)} %param.8, s32[4]{0:T(128)S(1)} %bitcast.155, s32[4]{0:T(128)S(1)} %bitcast_subtract_fusion.2), kind=kOutput, calls=%fused_computation.3 | convolution fusion | flops 30093312 | bytes 2371616 | tf_op jit(solution)/shard_map/dot_general | solution.py:68
  16.9 3.1 %copy.40 = f32[768,768]{0,1:T(8,128)} copy(f32[768,768]{1,0:T(8,128)} %add_multiply_fusion) | data formatting | bytes 4718592 | tf_op jit(solution)/shard_map/mul | solution.py:58
  19.9 2.7 %fusion.2 = bf16[768,768]{1,0:T(8,128)(2,1)S(1)} fusion(f32[768,768]{0,1:T(8,128)} %copy.40, f32[768]{0:T(1024)S(1)} %select_reduce_fusion, bf16[768,768]{1,0:T(8,128)(2,1)} %param.7), kind=kLoop, calls=%fused_computation.5 | loop fusion | flops 5308416 | bytes 4721664 | tf_op jit(solution)/shard_map/convert_element_type | solution.py:59
  30.7 3.9 %collective-permute-done.6 = bf16[128,768]{0,1:T(8,128)(2,1)S(1)} collective-permute-done((bf16[128,768]{0,1:T(8,128)(2,1)S(1)}, bf16[128,768]{0,1:T(8,128)(2,1)S(1)}, u32[]{:S(2)}, u32[]{:S(2)}) %collective-permute-start.6) | collective-permute-done | bytes 196640 | tf_op jit(solution)/shard_map/ppermute | solution.py:17
  35.1 2.9 %collective-permute-done.7 = bf16[128,768]{0,1:T(8,128)(2,1)S(1)} collective-permute-done((bf16[128,768]{0,1:T(8,128)(2,1)S(1)}, bf16[128,768]{0,1:T(8,128)(2,1)S(1)}, u32[]{:S(2)}, u32[]{:S(2)}) %collective-permute-start.7) | collective-permute-done | bytes 196640 | tf_op jit(solution)/shard_map/ppermute | solution.py:17
  42.9 2.7 %collective-permute-done.10 = bf16[128,768]{0,1:T(8,128)(2,1)S(1)} collective-permute-done((bf16[128,768]{0,1:T(8,128)(2,1)S(1)}, bf16[128,768]{0,1:T(8,128)(2,1)S(1)}, u32[]{:S(2)}, u32[]{:S(2)}) %collective-permute-start.10) | collective-permute-done | bytes 196640 | tf_op jit(solution)/shard_map/ppermute | solution.py:17
  46.1 3.2 %collective-permute-done.11 = bf16[128,768]{0,1:T(8,128)(2,1)S(1)} collective-permute-done((bf16[128,768]{0,1:T(8,128)(2,1)S(1)}, bf16[128,768]{0,1:T(8,128)(2,1)S(1)}, u32[]{:S(2)}, u32[]{:S(2)}) %collective-permute-start.11) | collective-permute-done | bytes 196640 | tf_op jit(solution)/shard_map/ppermute | solution.py:17
  54.3 4.0 %collective-permute-done.14 = bf16[128,768]{0,1:T(8,128)(2,1)S(1)} collective-permute-done((bf16[128,768]{0,1:T(8,128)(2,1)S(1)}, bf16[128,768]{0,1:T(8,128)(2,1)S(1)}, u32[]{:S(2)}, u32[]{:S(2)}) %collective-permute-start.14) | collective-permute-done | bytes 196640 | tf_op jit(solution)/shard_map/ppermute | solution.py:17
  58.8 2.4 %collective-permute-done.15 = bf16[128,768]{0,1:T(8,128)(2,1)S(1)} collective-permute-done((bf16[128,768]{0,1:T(8,128)(2,1)S(1)}, bf16[128,768]{0,1:T(8,128)(2,1)S(1)}, u32[]{:S(2)}, u32[]{:S(2)}) %collective-permute-start.15) | collective-permute-done | bytes 196640 | tf_op jit(solution)/shard_map/ppermute | solution.py:17
  66.4 3.0 %collective-permute-done.18 = bf16[128,768]{0,1:T(8,128)(2,1)S(1)} collective-permute-done((bf16[128,768]{0,1:T(8,128)(2,1)S(1)}, bf16[128,768]{0,1:T(8,128)(2,1)S(1)}, u32[]{:S(2)}, u32[]{:S(2)}) %collective-permute-start.18) | collective-permute-done | bytes 196640 | tf_op jit(solution)/shard_map/ppermute | solution.py:17
  77.2 3.1 %collective-permute-done.22 = bf16[128,768]{0,1:T(8,128)(2,1)S(1)} collective-permute-done((bf16[128,768]{0,1:T(8,128)(2,1)S(1)}, bf16[128,768]{0,1:T(8,128)(2,1)S(1)}, u32[]{:S(2)}, u32[]{:S(2)}) %collective-permute-start.22) | collective-permute-done | bytes 196640 | tf_op jit(solution)/shard_map/ppermute | solution.py:17
  80.8 2.5 %collective-permute-done.23 = bf16[128,768]{0,1:T(8,128)(2,1)S(1)} collective-permute-done((bf16[128,768]{0,1:T(8,128)(2,1)S(1)}, bf16[128,768]{0,1:T(8,128)(2,1)S(1)}, u32[]{:S(2)}, u32[]{:S(2)}) %collective-permute-start.23) | collective-permute-done | bytes 196640 | tf_op jit(solution)/shard_map/ppermute | solution.py:17
  91.0 3.3 %collective-permute-done.27 = bf16[128,768]{0,1:T(8,128)(2,1)S(1)} collective-permute-done((bf16[128,768]{0,1:T(8,128)(2,1)S(1)}, bf16[128,768]{0,1:T(8,128)(2,1)S(1)}, u32[]{:S(2)}, u32[]{:S(2)}) %collective-permute-start.27) | collective-permute-done | bytes 196640 | tf_op jit(solution)/shard_map/ppermute | solution.py:17
  99.2 4.7 %collective-permute-done.30 = bf16[128,768]{0,1:T(8,128)(2,1)S(1)} collective-permute-done((bf16[128,768]{0,1:T(8,128)(2,1)S(1)}, bf16[128,768]{0,1:T(8,128)(2,1)S(1)}, u32[]{:S(2)}, u32[]{:S(2)}) %collective-permute-start.30) | collective-permute-done | bytes 196640 | tf_op jit(solution)/shard_map/ppermute | solution.py:17
  104.4 2.4 %collective-permute-done.31 = bf16[128,768]{0,1:T(8,128)(2,1)S(1)} collective-permute-done((bf16[128,768]{0,1:T(8,128)(2,1)S(1)}, bf16[128,768]{0,1:T(8,128)(2,1)S(1)}, u32[]{:S(2)}, u32[]{:S(2)}) %collective-permute-start.31) | collective-permute-done | bytes 196640 | tf_op jit(solution)/shard_map/ppermute | solution.py:17
  107.3 18.9 %all_gather.12 = bf16[512,768]{0,1:T(8,128)(2,1)S(1)} all-gather(bf16[128,768]{0,1:T(8,128)(2,1)S(1)} %fusion.50), channel_id=1, replica_groups=mesh['atoms'=8,'bands'=4] {'bands'}, dimensions={0}, use_global_device_ids=true | all-gather | bytes 983040 | tf_op jit(solution)/shard_map/all_gather | solution.py:88
  126.6 11.8 %psum.28 = f32[128]{0:T(128)S(1)} all-reduce(f32[128]{0:T(128)S(1)} %get-tuple-element.22), channel_id=1, replica_groups=mesh['atoms'=8,'bands'=4] {'atoms'}, use_global_device_ids=true, to_apply=%region_5.6 | all-reduce | flops 128 | bytes 1024 | tf_op jit(solution)/shard_map/psum | solution.py:92
  138.5 17.6 %all_gather.13 = bf16[512,768]{0,1:T(8,128)(2,1)S(1)} all-gather(bf16[128,768]{0,1:T(8,128)(2,1)S(1)} %fusion.53), channel_id=1, replica_groups=mesh['atoms'=8,'bands'=4] {'bands'}, dimensions={0}, use_global_device_ids=true | all-gather | bytes 983040 | tf_op jit(solution)/shard_map/all_gather | solution.py:88
  156.4 11.8 %psum.29 = f32[128]{0:T(128)S(1)} all-reduce(f32[128]{0:T(128)S(1)} %get-tuple-element.24), channel_id=1, replica_groups=mesh['atoms'=8,'bands'=4] {'atoms'}, use_global_device_ids=true, to_apply=%region_7.8 | all-reduce | flops 128 | bytes 1024 | tf_op jit(solution)/shard_map/psum | solution.py:92
  168.3 17.6 %all_gather.14 = bf16[512,768]{0,1:T(8,128)(2,1)S(1)} all-gather(bf16[128,768]{0,1:T(8,128)(2,1)S(1)} %fusion.54), channel_id=1, replica_groups=mesh['atoms'=8,'bands'=4] {'bands'}, dimensions={0}, use_global_device_ids=true | all-gather | bytes 983040 | tf_op jit(solution)/shard_map/all_gather | solution.py:88
  186.2 11.8 %psum.30 = f32[128]{0:T(128)S(1)} all-reduce(f32[128]{0:T(128)S(1)} %get-tuple-element.26), channel_id=1, replica_groups=mesh['atoms'=8,'bands'=4] {'atoms'}, use_global_device_ids=true, to_apply=%region_9.10 | all-reduce | flops 128 | bytes 1024 | tf_op jit(solution)/shard_map/psum | solution.py:92
  198.1 17.6 %all_gather.15 = bf16[512,768]{0,1:T(8,128)(2,1)S(1)} all-gather(bf16[128,768]{0,1:T(8,128)(2,1)S(1)} %fusion.55), channel_id=1, replica_groups=mesh['atoms'=8,'bands'=4] {'bands'}, dimensions={0}, use_global_device_ids=true | all-gather | bytes 983040 | tf_op jit(solution)/shard_map/all_gather | solution.py:88
  216.0 11.8 %psum.31 = f32[128]{0:T(128)S(1)} all-reduce(f32[128]{0:T(128)S(1)} %get-tuple-element.28), channel_id=1, replica_groups=mesh['atoms'=8,'bands'=4] {'atoms'}, use_global_device_ids=true, to_apply=%region_11.12 | all-reduce | flops 128 | bytes 1024 | tf_op jit(solution)/shard_map/psum | solution.py:92
  (130 shorter events, 59.9 us)
Async XLA Ops:
  0.0 23.2 %collective-permute-start.2 = (bf16[128,768]{1,0:T(8,128)(2,1)}, bf16[128,768]{1,0:T(8,128)(2,1)}, u32[]{:S(2)}, u32[]{:S(2)}) collective-permute-start(bf16[128,768]{1,0:T(8,128)(2,1)} %param.6), channel_id=1, source_target_pairs={{0,8},{4,12},{8,0},{12,4},{16,24},{20,28},{24,16},{28,20},{1,9},{5... | collective-permute-start | bytes 589832 | tf_op jit(solution)/shard_map/ppermute | solution.py:17
  2.9 21.7 %collective-permute-start = (bf16[128,768]{1,0:T(8,128)(2,1)}, bf16[128,768]{1,0:T(8,128)(2,1)}, u32[]{:S(2)}, u32[]{:S(2)}) collective-permute-start(bf16[128,768]{1,0:T(8,128)(2,1)} %param.6), channel_id=1, source_target_pairs={{0,4},{4,0},{8,12},{12,8},{16,20},{20,16},{24,28},{28,24},{1,5},{5... | collective-permute-start | bytes 589832 | tf_op jit(solution)/shard_map/ppermute | solution.py:17
  9.6 15.1 %collective-permute-start.1 = (bf16[128,768]{0,1:T(8,128)(2,1)}, bf16[128,768]{0,1:T(8,128)(2,1)}, u32[]{:S(2)}, u32[]{:S(2)}) collective-permute-start(bf16[128,768]{0,1:T(8,128)(2,1)} %fusion.51), channel_id=1, source_target_pairs={{0,4},{4,0},{8,12},{12,8},{16,20},{20,16},{24,28},{28,24},{1,5},{5... | collective-permute-start | bytes 589832 | tf_op jit(solution)/shard_map/ppermute | solution.py:17
  13.0 11.6 %collective-permute-start.3 = (bf16[128,768]{0,1:T(8,128)(2,1)}, bf16[128,768]{0,1:T(8,128)(2,1)}, u32[]{:S(2)}, u32[]{:S(2)}) collective-permute-start(bf16[128,768]{0,1:T(8,128)(2,1)} %fusion.52), channel_id=1, source_target_pairs={{0,8},{4,12},{8,0},{12,4},{16,24},{20,28},{24,16},{28,20},{1,9},{5... | collective-permute-start | bytes 589832 | tf_op jit(solution)/shard_map/ppermute | solution.py:17
  26.9 7.7 %collective-permute-start.6 = (bf16[128,768]{0,1:T(8,128)(2,1)S(1)}, bf16[128,768]{0,1:T(8,128)(2,1)S(1)}, u32[]{:S(2)}, u32[]{:S(2)}) collective-permute-start(bf16[128,768]{0,1:T(8,128)(2,1)S(1)} %get-tuple-element.8), channel_id=1, source_target_pairs={{0,8},{4,12},{8,0},{12,4},{16,24},{20,28},{24,16},{28,20},{1,9},{5... | collective-permute-start | bytes 589832 | tf_op jit(solution)/shard_map/ppermute | solution.py:17
  29.6 8.4 %collective-permute-start.4 = (bf16[128,768]{0,1:T(8,128)(2,1)S(1)}, bf16[128,768]{0,1:T(8,128)(2,1)S(1)}, u32[]{:S(2)}, u32[]{:S(2)}) collective-permute-start(bf16[128,768]{0,1:T(8,128)(2,1)S(1)} %get-tuple-element.8), channel_id=1, source_target_pairs={{0,4},{4,0},{8,12},{12,8},{16,20},{20,16},{24,28},{28,24},{1,5},{5... | collective-permute-start | bytes 589832 | tf_op jit(solution)/shard_map/ppermute | solution.py:17
  30.1 7.8 %collective-permute-start.7 = (bf16[128,768]{0,1:T(8,128)(2,1)S(1)}, bf16[128,768]{0,1:T(8,128)(2,1)S(1)}, u32[]{:S(2)}, u32[]{:S(2)}) collective-permute-start(bf16[128,768]{0,1:T(8,128)(2,1)S(1)} %convolution_convert_fusion.12), channel_id=1, source_target_pairs={{0,8},{4,12},{8,0},{12,4},{16,24},{20,28},{24,16},{28,20},{1,9},{5... | collective-permute-start | bytes 589832 | tf_op jit(solution)/shard_map/ppermute | solution.py:17
  41.4 7.9 %collective-permute-start.8 = (bf16[128,768]{0,1:T(8,128)(2,1)S(1)}, bf16[128,768]{0,1:T(8,128)(2,1)S(1)}, u32[]{:S(2)}, u32[]{:S(2)}) collective-permute-start(bf16[128,768]{0,1:T(8,128)(2,1)S(1)} %get-tuple-element.10), channel_id=1, source_target_pairs={{0,4},{4,0},{8,12},{12,8},{16,20},{20,16},{24,28},{28,24},{1,5},{5... | collective-permute-start | bytes 589832 | tf_op jit(solution)/shard_map/ppermute | solution.py:17
  42.0 7.4 %collective-permute-start.11 = (bf16[128,768]{0,1:T(8,128)(2,1)S(1)}, bf16[128,768]{0,1:T(8,128)(2,1)S(1)}, u32[]{:S(2)}, u32[]{:S(2)}) collective-permute-start(bf16[128,768]{0,1:T(8,128)(2,1)S(1)} %convolution_convert_fusion.10), channel_id=1, source_target_pairs={{0,8},{4,12},{8,0},{12,4},{16,24},{20,28},{24,16},{28,20},{1,9},{5... | collective-permute-start | bytes 589832 | tf_op jit(solution)/shard_map/ppermute | solution.py:17
  50.5 7.9 %collective-permute-start.14 = (bf16[128,768]{0,1:T(8,128)(2,1)S(1)}, bf16[128,768]{0,1:T(8,128)(2,1)S(1)}, u32[]{:S(2)}, u32[]{:S(2)}) collective-permute-start(bf16[128,768]{0,1:T(8,128)(2,1)S(1)} %get-tuple-element.12), channel_id=1, source_target_pairs={{0,8},{4,12},{8,0},{12,4},{16,24},{20,28},{24,16},{28,20},{1,9},{5... | collective-permute-start | bytes 589832 | tf_op jit(solution)/shard_map/ppermute | solution.py:17
  52.5 8.8 %collective-permute-start.12 = (bf16[128,768]{0,1:T(8,128)(2,1)S(1)}, bf16[128,768]{0,1:T(8,128)(2,1)S(1)}, u32[]{:S(2)}, u32[]{:S(2)}) collective-permute-start(bf16[128,768]{0,1:T(8,128)(2,1)S(1)} %get-tuple-element.12), channel_id=1, source_target_pairs={{0,4},{4,0},{8,12},{12,8},{16,20},{20,16},{24,28},{28,24},{1,5},{5... | collective-permute-start | bytes 589832 | tf_op jit(solution)/shard_map/ppermute | solution.py:17
  53.1 8.2 %collective-permute-start.15 = (bf16[128,768]{0,1:T(8,128)(2,1)S(1)}, bf16[128,768]{0,1:T(8,128)(2,1)S(1)}, u32[]{:S(2)}, u32[]{:S(2)}) collective-permute-start(bf16[128,768]{0,1:T(8,128)(2,1)S(1)} %convolution_convert_fusion.8), channel_id=1, source_target_pairs={{0,8},{4,12},{8,0},{12,4},{16,24},{20,28},{24,16},{28,20},{1,9},{5... | collective-permute-start | bytes 589832 | tf_op jit(solution)/shard_map/ppermute | solution.py:17
  62.3 7.1 %collective-permute-start.18 = (bf16[128,768]{0,1:T(8,128)(2,1)S(1)}, bf16[128,768]{0,1:T(8,128)(2,1)S(1)}, u32[]{:S(2)}, u32[]{:S(2)}) collective-permute-start(bf16[128,768]{0,1:T(8,128)(2,1)S(1)} %get-tuple-element.14), channel_id=1, source_target_pairs={{0,8},{4,12},{8,0},{12,4},{16,24},{20,28},{24,16},{28,20},{1,9},{5... | collective-permute-start | bytes 589832 | tf_op jit(solution)/shard_map/ppermute | solution.py:17
  63.5 8.8 %collective-permute-start.16 = (bf16[128,768]{0,1:T(8,128)(2,1)S(1)}, bf16[128,768]{0,1:T(8,128)(2,1)S(1)}, u32[]{:S(2)}, u32[]{:S(2)}) collective-permute-start(bf16[128,768]{0,1:T(8,128)(2,1)S(1)} %get-tuple-element.14), channel_id=1, source_target_pairs={{0,4},{4,0},{8,12},{12,8},{16,20},{20,16},{24,28},{28,24},{1,5},{5... | collective-permute-start | bytes 589832 | tf_op jit(solution)/shard_map/ppermute | solution.py:17
  64.1 8.2 %collective-permute-start.19 = (bf16[128,768]{0,1:T(8,128)(2,1)S(1)}, bf16[128,768]{0,1:T(8,128)(2,1)S(1)}, u32[]{:S(2)}, u32[]{:S(2)}) collective-permute-start(bf16[128,768]{0,1:T(8,128)(2,1)S(1)} %convolution_convert_fusion.6), channel_id=1, source_target_pairs={{0,8},{4,12},{8,0},{12,4},{16,24},{20,28},{24,16},{28,20},{1,9},{5... | collective-permute-start | bytes 589832 | tf_op jit(solution)/shard_map/ppermute | solution.py:17
  73.4 7.0 %collective-permute-start.22 = (bf16[128,768]{0,1:T(8,128)(2,1)S(1)}, bf16[128,768]{0,1:T(8,128)(2,1)S(1)}, u32[]{:S(2)}, u32[]{:S(2)}) collective-permute-start(bf16[128,768]{0,1:T(8,128)(2,1)S(1)} %get-tuple-element.16), channel_id=1, source_target_pairs={{0,8},{4,12},{8,0},{12,4},{16,24},{20,28},{24,16},{28,20},{1,9},{5... | collective-permute-start | bytes 589832 | tf_op jit(solution)/shard_map/ppermute | solution.py:17
  74.6 8.7 %collective-permute-start.20 = (bf16[128,768]{0,1:T(8,128)(2,1)S(1)}, bf16[128,768]{0,1:T(8,128)(2,1)S(1)}, u32[]{:S(2)}, u32[]{:S(2)}) collective-permute-start(bf16[128,768]{0,1:T(8,128)(2,1)S(1)} %get-tuple-element.16), channel_id=1, source_target_pairs={{0,4},{4,0},{8,12},{12,8},{16,20},{20,16},{24,28},{28,24},{1,5},{5... | collective-permute-start | bytes 589832 | tf_op jit(solution)/shard_map/ppermute | solution.py:17
  75.2 8.1 %collective-permute-start.23 = (bf16[128,768]{0,1:T(8,128)(2,1)S(1)}, bf16[128,768]{0,1:T(8,128)(2,1)S(1)}, u32[]{:S(2)}, u32[]{:S(2)}) collective-permute-start(bf16[128,768]{0,1:T(8,128)(2,1)S(1)} %convolution_convert_fusion.4), channel_id=1, source_target_pairs={{0,8},{4,12},{8,0},{12,4},{16,24},{20,28},{24,16},{28,20},{1,9},{5... | collective-permute-start | bytes 589832 | tf_op jit(solution)/shard_map/ppermute | solution.py:17
  86.4 7.9 %collective-permute-start.24 = (bf16[128,768]{0,1:T(8,128)(2,1)S(1)}, bf16[128,768]{0,1:T(8,128)(2,1)S(1)}, u32[]{:S(2)}, u32[]{:S(2)}) collective-permute-start(bf16[128,768]{0,1:T(8,128)(2,1)S(1)} %get-tuple-element.18), channel_id=1, source_target_pairs={{0,4},{4,0},{8,12},{12,8},{16,20},{20,16},{24,28},{28,24},{1,5},{5... | collective-permute-start | bytes 589832 | tf_op jit(solution)/shard_map/ppermute | solution.py:17
  87.0 7.3 %collective-permute-start.27 = (bf16[128,768]{0,1:T(8,128)(2,1)S(1)}, bf16[128,768]{0,1:T(8,128)(2,1)S(1)}, u32[]{:S(2)}, u32[]{:S(2)}) collective-permute-start(bf16[128,768]{0,1:T(8,128)(2,1)S(1)} %convolution_convert_fusion.2), channel_id=1, source_target_pairs={{0,8},{4,12},{8,0},{12,4},{16,24},{20,28},{24,16},{28,20},{1,9},{5... | collective-permute-start | bytes 589832 | tf_op jit(solution)/shard_map/ppermute | solution.py:17
  96.0 7.9 %collective-permute-start.30 = (bf16[128,768]{0,1:T(8,128)(2,1)S(1)}, bf16[128,768]{0,1:T(8,128)(2,1)S(1)}, u32[]{:S(2)}, u32[]{:S(2)}) collective-permute-start(bf16[128,768]{0,1:T(8,128)(2,1)S(1)} %get-tuple-element.20), channel_id=1, source_target_pairs={{0,8},{4,12},{8,0},{12,4},{16,24},{20,28},{24,16},{28,20},{1,9},{5... | collective-permute-start | bytes 589832 | tf_op jit(solution)/shard_map/ppermute | solution.py:17
  97.6 9.2 %collective-permute-start.28 = (bf16[128,768]{0,1:T(8,128)(2,1)S(1)}, bf16[128,768]{0,1:T(8,128)(2,1)S(1)}, u32[]{:S(2)}, u32[]{:S(2)}) collective-permute-start(bf16[128,768]{0,1:T(8,128)(2,1)S(1)} %get-tuple-element.20), channel_id=1, source_target_pairs={{0,4},{4,0},{8,12},{12,8},{16,20},{20,16},{24,28},{28,24},{1,5},{5... | collective-permute-start | bytes 589832 | tf_op jit(solution)/shard_map/ppermute | solution.py:17
  97.6 6.8 %collective-permute-start.29 = (bf16[128,768]{0,1:T(8,128)(2,1)S(1)}, bf16[128,768]{0,1:T(8,128)(2,1)S(1)}, u32[]{:S(2)}, u32[]{:S(2)}) collective-permute-start(bf16[128,768]{0,1:T(8,128)(2,1)S(1)} %convolution_convert_fusion.1), channel_id=1, source_target_pairs={{0,4},{4,0},{8,12},{12,8},{16,20},{20,16},{24,28},{28,24},{1,5},{5... | collective-permute-start | bytes 589832 | tf_op jit(solution)/shard_map/ppermute | solution.py:17
  98.1 8.7 %collective-permute-start.31 = (bf16[128,768]{0,1:T(8,128)(2,1)S(1)}, bf16[128,768]{0,1:T(8,128)(2,1)S(1)}, u32[]{:S(2)}, u32[]{:S(2)}) collective-permute-start(bf16[128,768]{0,1:T(8,128)(2,1)S(1)} %convolution_convert_fusion), channel_id=1, source_target_pairs={{0,8},{4,12},{8,0},{12,4},{16,24},{20,28},{24,16},{28,20},{1,9},{5... | collective-permute-start | bytes 589832 | tf_op jit(solution)/shard_map/ppermute | solution.py:17
  (15 other events, 82.0 us)
where the time goes:
time: 229 us
  blocking collectives  119 us (52%)
  waiting for transfers between devices  42.9 us (19%)
  matrix products  32.2 us (14%)
  starting transfers between devices  22 us (10%)
  local copies, waits for them, and re-layouts  6.76 us (3%)
  other arithmetic  5.57 us (2%)
    all_gather x4, blocking collectives, body(): lax.all_gather(rounded, 'bands', axis=0, tiled=True)  71.6 us
    psum x4, blocking collectives, body(): squares = lax.psum(jnp.sum(mixed_rows * mixed_rows, axis=1), 'atoms')  47.2 us
    ppermute x32, waiting for transfers between devices, swapped(): return lax.ppermute(value, axis, pairs)  42.9 us
    ppermute x32, starting transfers between devices, swapped(): return lax.ppermute(value, axis, pairs)  22 us
    dot_general x16, matrix products, apply_operator(): sent_term = jnp.dot(values, pair_mat, preferred_element_type=jnp.float32)  10.7 us
    dot_general x16, matrix products, apply_operator(): lax.dot_general(other_rows, pair_mat, (((1,), (1,)), ((), ())), preferred...  9.66 us
    dot_general x8, matrix products, apply_operator(): result = jnp.dot(values, diag_sym, preferred_element_type=jnp.float32)  4.85 us
  transfers between devices with their start and end apart: 32, of which 14 were waited for; matrix products, arithmetic and copies ran while one was open for 14% of the time, Pallas kernels for 0%

commit v1 on v0

--- a/solution.py
+++ b/solution.py
@@ -89,7 +89,9 @@
             (((0,), (0,)), ((), ())),
             preferred_element_type=jnp.float32,
         )
-        squares = lax.psum(jnp.sum(mixed_rows * mixed_rows, axis=1), "atoms")
+        squares = jax.lax.all_gather(
+            jnp.sum(mixed_rows * mixed_rows, axis=1), axis_name="atoms"
+        ).sum(axis=0)
         col_norm = jnp.sqrt(squares / total_orbitals + norm_eps)
         basis_rows = mixed_rows / col_norm[:, None]
     return basis_rows

time: 229 us -> 216 us (0.943)
  blocking collectives: 119 us -> 106 us
    psum x4 -> x0, blocking collectives: 47.2 us -> none  [body(): squares = lax.psum(jnp.sum(mixed_rows * mixed_rows, axis=1), 'atoms')]
    all_gather x0 -> x4, blocking collectives: none -> 33 us  [body(): jax.lax.all_gather(jnp.sum(mixed_rows * mixed_rows, axis=1), axis_name='a...]
  transfers between devices with their start and end apart: 32 -> 32, of which waited for: 14 -> 14; matrix products, arithmetic and copies ran while one was open for 14% -> 15% of each run, Pallas kernels for 0% -> 0%
where the time goes in v1:
time: 216 us
  blocking collectives  106 us (49%)
  waiting for transfers between devices  42.9 us (20%)
  matrix products  31.7 us (15%)
  starting transfers between devices  22 us (10%)
  local copies, waits for them, and re-layouts  6.76 us (3%)
  other arithmetic  5.68 us (3%)
    all_gather x4, blocking collectives, body(): lax.all_gather(rounded, 'bands', axis=0, tiled=True)  73 us
    ppermute x32, waiting for transfers between devices, swapped(): return lax.ppermute(value, axis, pairs)  42.9 us
    all_gather x4, blocking collectives, body(): jax.lax.all_gather(jnp.sum(mixed_rows * mixed_rows, axis=1), axis_name='a...  33 us
    ppermute x32, starting transfers between devices, swapped(): return lax.ppermute(value, axis, pairs)  22 us
    dot_general x16, matrix products, apply_operator(): sent_term = jnp.dot(values, pair_mat, preferred_element_type=jnp.float32)  10.7 us
    dot_general x16, matrix products, apply_operator(): lax.dot_general(other_rows, pair_mat, (((1,), (1,)), ((), ())), preferred...  9.66 us
    dot_general x8, matrix products, apply_operator(): result = jnp.dot(values, diag_sym, preferred_element_type=jnp.float32)  4.84 us
  transfers between devices with their start and end apart: 32, of which 14 were waited for; matrix products, arithmetic and copies ran while one was open for 15% of the time, Pallas kernels for 0%

profile of v1, /device:TPU:0, one launch (start us, length us, event | category | flops | bytes accessed | tf_op | source)
XLA Modules:
  0.0 215.5 jit_solution(8909072356684999018)
XLA Ops:
  0.0 2.9 %collective-permute-start.2 = (bf16[128,768]{1,0:T(8,128)(2,1)}, bf16[128,768]{1,0:T(8,128)(2,1)}, u32[]{:S(2)}, u32[]{:S(2)}) collective-permute-start(bf16[128,768]{1,0:T(8,128)(2,1)} %param.6), channel_id=1, source_target_pairs={{0,8},{4,12},{8,0},{12,4},{16,24},{20,28},{24,16},{28,20},{1,9},{5... | collective-permute-start | bytes 589832 | tf_op jit(solution)/shard_map/ppermute | solution.py:17
  5.4 2.7 %fusion.1 = bf16[768,768]{1,0:T(8,128)(2,1)S(1)} fusion(f32[768,4]{0,1:T(4,128)S(1)} %fusion.70, bf16[2,768,768]{2,1,0:T(8,128)(2,1)} %param.8, s32[4]{0:T(128)S(1)} %bitcast.159, s32[4]{0:T(128)S(1)} %bitcast_subtract_fusion.2), kind=kOutput, calls=%fused_computation.3 | convolution fusion | flops 30090240 | bytes 2371616 | tf_op jit(solution)/shard_map/dot_general | solution.py:68
  16.3 3.1 %copy.73 = f32[768,768]{0,1:T(8,128)} copy(f32[768,768]{1,0:T(8,128)} %add_multiply_fusion) | data formatting | bytes 4718592 | tf_op jit(solution)/shard_map/mul | solution.py:58
  19.4 2.7 %fusion.2 = bf16[768,768]{1,0:T(8,128)(2,1)S(1)} fusion(f32[768,768]{0,1:T(8,128)} %copy.73, f32[768]{0:T(1024)S(1)} %select_reduce_fusion, bf16[768,768]{1,0:T(8,128)(2,1)} %param.7), kind=kLoop, calls=%fused_computation.5 | loop fusion | flops 5308416 | bytes 4721664 | tf_op jit(solution)/shard_map/convert_element_type | solution.py:59
  30.2 3.9 %collective-permute-done.6 = bf16[128,768]{0,1:T(8,128)(2,1)S(1)} collective-permute-done((bf16[128,768]{0,1:T(8,128)(2,1)S(1)}, bf16[128,768]{0,1:T(8,128)(2,1)S(1)}, u32[]{:S(2)}, u32[]{:S(2)}) %collective-permute-start.6) | collective-permute-done | bytes 196640 | tf_op jit(solution)/shard_map/ppermute | solution.py:17
  34.6 2.8 %collective-permute-done.7 = bf16[128,768]{0,1:T(8,128)(2,1)S(1)} collective-permute-done((bf16[128,768]{0,1:T(8,128)(2,1)S(1)}, bf16[128,768]{0,1:T(8,128)(2,1)S(1)}, u32[]{:S(2)}, u32[]{:S(2)}) %collective-permute-start.7) | collective-permute-done | bytes 196640 | tf_op jit(solution)/shard_map/ppermute | solution.py:17
  42.4 2.7 %collective-permute-done.10 = bf16[128,768]{0,1:T(8,128)(2,1)S(1)} collective-permute-done((bf16[128,768]{0,1:T(8,128)(2,1)S(1)}, bf16[128,768]{0,1:T(8,128)(2,1)S(1)}, u32[]{:S(2)}, u32[]{:S(2)}) %collective-permute-start.10) | collective-permute-done | bytes 196640 | tf_op jit(solution)/shard_map/ppermute | solution.py:17
  45.6 3.2 %collective-permute-done.11 = bf16[128,768]{0,1:T(8,128)(2,1)S(1)} collective-permute-done((bf16[128,768]{0,1:T(8,128)(2,1)S(1)}, bf16[128,768]{0,1:T(8,128)(2,1)S(1)}, u32[]{:S(2)}, u32[]{:S(2)}) %collective-permute-start.11) | collective-permute-done | bytes 196640 | tf_op jit(solution)/shard_map/ppermute | solution.py:17
  53.8 3.9 %collective-permute-done.14 = bf16[128,768]{0,1:T(8,128)(2,1)S(1)} collective-permute-done((bf16[128,768]{0,1:T(8,128)(2,1)S(1)}, bf16[128,768]{0,1:T(8,128)(2,1)S(1)}, u32[]{:S(2)}, u32[]{:S(2)}) %collective-permute-start.14) | collective-permute-done | bytes 196640 | tf_op jit(solution)/shard_map/ppermute | solution.py:17
  58.1 2.5 %collective-permute-done.15 = bf16[128,768]{0,1:T(8,128)(2,1)S(1)} collective-permute-done((bf16[128,768]{0,1:T(8,128)(2,1)S(1)}, bf16[128,768]{0,1:T(8,128)(2,1)S(1)}, u32[]{:S(2)}, u32[]{:S(2)}) %collective-permute-start.15) | collective-permute-done | bytes 196640 | tf_op jit(solution)/shard_map/ppermute | solution.py:17
  65.8 3.0 %collective-permute-done.18 = bf16[128,768]{0,1:T(8,128)(2,1)S(1)} collective-permute-done((bf16[128,768]{0,1:T(8,128)(2,1)S(1)}, bf16[128,768]{0,1:T(8,128)(2,1)S(1)}, u32[]{:S(2)}, u32[]{:S(2)}) %collective-permute-start.18) | collective-permute-done | bytes 196640 | tf_op jit(solution)/shard_map/ppermute | solution.py:17
  76.7 3.2 %collective-permute-done.22 = bf16[128,768]{0,1:T(8,128)(2,1)S(1)} collective-permute-done((bf16[128,768]{0,1:T(8,128)(2,1)S(1)}, bf16[128,768]{0,1:T(8,128)(2,1)S(1)}, u32[]{:S(2)}, u32[]{:S(2)}) %collective-permute-start.22) | collective-permute-done | bytes 196640 | tf_op jit(solution)/shard_map/ppermute | solution.py:17
  80.3 2.4 %collective-permute-done.23 = bf16[128,768]{0,1:T(8,128)(2,1)S(1)} collective-permute-done((bf16[128,768]{0,1:T(8,128)(2,1)S(1)}, bf16[128,768]{0,1:T(8,128)(2,1)S(1)}, u32[]{:S(2)}, u32[]{:S(2)}) %collective-permute-start.23) | collective-permute-done | bytes 196640 | tf_op jit(solution)/shard_map/ppermute | solution.py:17
  90.5 3.3 %collective-permute-done.27 = bf16[128,768]{0,1:T(8,128)(2,1)S(1)} collective-permute-done((bf16[128,768]{0,1:T(8,128)(2,1)S(1)}, bf16[128,768]{0,1:T(8,128)(2,1)S(1)}, u32[]{:S(2)}, u32[]{:S(2)}) %collective-permute-start.27) | collective-permute-done | bytes 196640 | tf_op jit(solution)/shard_map/ppermute | solution.py:17
  98.7 4.7 %collective-permute-done.30 = bf16[128,768]{0,1:T(8,128)(2,1)S(1)} collective-permute-done((bf16[128,768]{0,1:T(8,128)(2,1)S(1)}, bf16[128,768]{0,1:T(8,128)(2,1)S(1)}, u32[]{:S(2)}, u32[]{:S(2)}) %collective-permute-start.30) | collective-permute-done | bytes 196640 | tf_op jit(solution)/shard_map/ppermute | solution.py:17
  103.9 2.4 %collective-permute-done.31 = bf16[128,768]{0,1:T(8,128)(2,1)S(1)} collective-permute-done((bf16[128,768]{0,1:T(8,128)(2,1)S(1)}, bf16[128,768]{0,1:T(8,128)(2,1)S(1)}, u32[]{:S(2)}, u32[]{:S(2)}) %collective-permute-start.31) | collective-permute-done | bytes 196640 | tf_op jit(solution)/shard_map/ppermute | solution.py:17
  106.8 18.9 %all_gather.36 = bf16[512,768]{0,1:T(8,128)(2,1)S(1)} all-gather(bf16[128,768]{0,1:T(8,128)(2,1)S(1)} %fusion.50), channel_id=1, replica_groups=mesh['atoms'=8,'bands'=4] {'bands'}, dimensions={0}, use_global_device_ids=true | all-gather | bytes 983040 | tf_op jit(solution)/shard_map/all_gather | solution.py:88
  126.1 8.8 %all-gather.4 = f32[8,1,128]{2,1,0:T(1,128)S(1)} all-gather(f32[1,1,128]{2,1,0:T(1,128)S(1)} %bitcast.162), channel_id=2, replica_groups=mesh['atoms'=8,'bands'=4] {'atoms'}, dimensions={0}, use_global_device_ids=true | all-gather | bytes 4608 | tf_op jit(solution)/shard_map/all_gather | solution.py:92
  134.9 18.0 %all_gather.39 = bf16[512,768]{0,1:T(8,128)(2,1)S(1)} all-gather(bf16[128,768]{0,1:T(8,128)(2,1)S(1)} %fusion.53), channel_id=1, replica_groups=mesh['atoms'=8,'bands'=4] {'bands'}, dimensions={0}, use_global_device_ids=true | all-gather | bytes 983040 | tf_op jit(solution)/shard_map/all_gather | solution.py:88
  153.3 7.7 %all-gather.5 = f32[8,1,128]{2,1,0:T(1,128)S(1)} all-gather(f32[1,1,128]{2,1,0:T(1,128)S(1)} %bitcast.163), channel_id=3, replica_groups=mesh['atoms'=8,'bands'=4] {'atoms'}, dimensions={0}, use_global_device_ids=true | all-gather | bytes 4608 | tf_op jit(solution)/shard_map/all_gather | solution.py:92
  161.2 18.0 %all_gather.42 = bf16[512,768]{0,1:T(8,128)(2,1)S(1)} all-gather(bf16[128,768]{0,1:T(8,128)(2,1)S(1)} %fusion.54), channel_id=1, replica_groups=mesh['atoms'=8,'bands'=4] {'bands'}, dimensions={0}, use_global_device_ids=true | all-gather | bytes 983040 | tf_op jit(solution)/shard_map/all_gather | solution.py:88
  179.5 8.8 %all-gather.6 = f32[8,1,128]{2,1,0:T(1,128)S(1)} all-gather(f32[1,1,128]{2,1,0:T(1,128)S(1)} %bitcast.164), channel_id=4, replica_groups=mesh['atoms'=8,'bands'=4] {'atoms'}, dimensions={0}, use_global_device_ids=true | all-gather | bytes 4608 | tf_op jit(solution)/shard_map/all_gather | solution.py:92
  188.4 18.0 %all_gather.45 = bf16[512,768]{0,1:T(8,128)(2,1)S(1)} all-gather(bf16[128,768]{0,1:T(8,128)(2,1)S(1)} %fusion.55), channel_id=1, replica_groups=mesh['atoms'=8,'bands'=4] {'bands'}, dimensions={0}, use_global_device_ids=true | all-gather | bytes 983040 | tf_op jit(solution)/shard_map/all_gather | solution.py:88
  206.8 7.8 %all-gather.7 = f32[8,1,128]{2,1,0:T(1,128)S(1)} all-gather(f32[1,1,128]{2,1,0:T(1,128)S(1)} %bitcast.165), channel_id=5, replica_groups=mesh['atoms'=8,'bands'=4] {'atoms'}, dimensions={0}, use_global_device_ids=true | all-gather | bytes 4608 | tf_op jit(solution)/shard_map/all_gather | solution.py:92
  (134 shorter events, 59.4 us)
Async XLA Ops:
  0.0 22.7 %collective-permute-start.2 = (bf16[128,768]{1,0:T(8,128)(2,1)}, bf16[128,768]{1,0:T(8,128)(2,1)}, u32[]{:S(2)}, u32[]{:S(2)}) collective-permute-start(bf16[128,768]{1,0:T(8,128)(2,1)} %param.6), channel_id=1, source_target_pairs={{0,8},{4,12},{8,0},{12,4},{16,24},{20,28},{24,16},{28,20},{1,9},{5... | collective-permute-start | bytes 589832 | tf_op jit(solution)/shard_map/ppermute | solution.py:17
  2.9 21.2 %collective-permute-start = (bf16[128,768]{1,0:T(8,128)(2,1)}, bf16[128,768]{1,0:T(8,128)(2,1)}, u32[]{:S(2)}, u32[]{:S(2)}) collective-permute-start(bf16[128,768]{1,0:T(8,128)(2,1)} %param.6), channel_id=1, source_target_pairs={{0,4},{4,0},{8,12},{12,8},{16,20},{20,16},{24,28},{28,24},{1,5},{5... | collective-permute-start | bytes 589832 | tf_op jit(solution)/shard_map/ppermute | solution.py:17
  9.3 14.8 %collective-permute-start.1 = (bf16[128,768]{0,1:T(8,128)(2,1)}, bf16[128,768]{0,1:T(8,128)(2,1)}, u32[]{:S(2)}, u32[]{:S(2)}) collective-permute-start(bf16[128,768]{0,1:T(8,128)(2,1)} %fusion.51), channel_id=1, source_target_pairs={{0,4},{4,0},{8,12},{12,8},{16,20},{20,16},{24,28},{28,24},{1,5},{5... | collective-permute-start | bytes 589832 | tf_op jit(solution)/shard_map/ppermute | solution.py:17
  12.5 11.6 %collective-permute-start.3 = (bf16[128,768]{0,1:T(8,128)(2,1)}, bf16[128,768]{0,1:T(8,128)(2,1)}, u32[]{:S(2)}, u32[]{:S(2)}) collective-permute-start(bf16[128,768]{0,1:T(8,128)(2,1)} %fusion.52), channel_id=1, source_target_pairs={{0,8},{4,12},{8,0},{12,4},{16,24},{20,28},{24,16},{28,20},{1,9},{5... | collective-permute-start | bytes 589832 | tf_op jit(solution)/shard_map/ppermute | solution.py:17
  26.3 7.8 %collective-permute-start.6 = (bf16[128,768]{0,1:T(8,128)(2,1)S(1)}, bf16[128,768]{0,1:T(8,128)(2,1)S(1)}, u32[]{:S(2)}, u32[]{:S(2)}) collective-permute-start(bf16[128,768]{0,1:T(8,128)(2,1)S(1)} %get-tuple-element.8), channel_id=1, source_target_pairs={{0,8},{4,12},{8,0},{12,4},{16,24},{20,28},{24,16},{28,20},{1,9},{5... | collective-permute-start | bytes 589832 | tf_op jit(solution)/shard_map/ppermute | solution.py:17
  29.0 8.4 %collective-permute-start.4 = (bf16[128,768]{0,1:T(8,128)(2,1)S(1)}, bf16[128,768]{0,1:T(8,128)(2,1)S(1)}, u32[]{:S(2)}, u32[]{:S(2)}) collective-permute-start(bf16[128,768]{0,1:T(8,128)(2,1)S(1)} %get-tuple-element.8), channel_id=1, source_target_pairs={{0,4},{4,0},{8,12},{12,8},{16,20},{20,16},{24,28},{28,24},{1,5},{5... | collective-permute-start | bytes 589832 | tf_op jit(solution)/shard_map/ppermute | solution.py:17
  29.6 7.8 %collective-permute-start.7 = (bf16[128,768]{0,1:T(8,128)(2,1)S(1)}, bf16[128,768]{0,1:T(8,128)(2,1)S(1)}, u32[]{:S(2)}, u32[]{:S(2)}) collective-permute-start(bf16[128,768]{0,1:T(8,128)(2,1)S(1)} %convolution_convert_fusion.12), channel_id=1, source_target_pairs={{0,8},{4,12},{8,0},{12,4},{16,24},{20,28},{24,16},{28,20},{1,9},{5... | collective-permute-start | bytes 589832 | tf_op jit(solution)/shard_map/ppermute | solution.py:17
  40.9 7.9 %collective-permute-start.8 = (bf16[128,768]{0,1:T(8,128)(2,1)S(1)}, bf16[128,768]{0,1:T(8,128)(2,1)S(1)}, u32[]{:S(2)}, u32[]{:S(2)}) collective-permute-start(bf16[128,768]{0,1:T(8,128)(2,1)S(1)} %get-tuple-element.10), channel_id=1, source_target_pairs={{0,4},{4,0},{8,12},{12,8},{16,20},{20,16},{24,28},{28,24},{1,5},{5... | collective-permute-start | bytes 589832 | tf_op jit(solution)/shard_map/ppermute | solution.py:17
  41.5 7.3 %collective-permute-start.11 = (bf16[128,768]{0,1:T(8,128)(2,1)S(1)}, bf16[128,768]{0,1:T(8,128)(2,1)S(1)}, u32[]{:S(2)}, u32[]{:S(2)}) collective-permute-start(bf16[128,768]{0,1:T(8,128)(2,1)S(1)} %convolution_convert_fusion.10), channel_id=1, source_target_pairs={{0,8},{4,12},{8,0},{12,4},{16,24},{20,28},{24,16},{28,20},{1,9},{5... | collective-permute-start | bytes 589832 | tf_op jit(solution)/shard_map/ppermute | solution.py:17
  49.9 7.7 %collective-permute-start.14 = (bf16[128,768]{0,1:T(8,128)(2,1)S(1)}, bf16[128,768]{0,1:T(8,128)(2,1)S(1)}, u32[]{:S(2)}, u32[]{:S(2)}) collective-permute-start(bf16[128,768]{0,1:T(8,128)(2,1)S(1)} %get-tuple-element.12), channel_id=1, source_target_pairs={{0,8},{4,12},{8,0},{12,4},{16,24},{20,28},{24,16},{28,20},{1,9},{5... | collective-permute-start | bytes 589832 | tf_op jit(solution)/shard_map/ppermute | solution.py:17
  51.9 8.7 %collective-permute-start.12 = (bf16[128,768]{0,1:T(8,128)(2,1)S(1)}, bf16[128,768]{0,1:T(8,128)(2,1)S(1)}, u32[]{:S(2)}, u32[]{:S(2)}) collective-permute-start(bf16[128,768]{0,1:T(8,128)(2,1)S(1)} %get-tuple-element.12), channel_id=1, source_target_pairs={{0,4},{4,0},{8,12},{12,8},{16,20},{20,16},{24,28},{28,24},{1,5},{5... | collective-permute-start | bytes 589832 | tf_op jit(solution)/shard_map/ppermute | solution.py:17
  52.5 8.1 %collective-permute-start.15 = (bf16[128,768]{0,1:T(8,128)(2,1)S(1)}, bf16[128,768]{0,1:T(8,128)(2,1)S(1)}, u32[]{:S(2)}, u32[]{:S(2)}) collective-permute-start(bf16[128,768]{0,1:T(8,128)(2,1)S(1)} %convolution_convert_fusion.8), channel_id=1, source_target_pairs={{0,8},{4,12},{8,0},{12,4},{16,24},{20,28},{24,16},{28,20},{1,9},{5... | collective-permute-start | bytes 589832 | tf_op jit(solution)/shard_map/ppermute | solution.py:17
  61.8 7.1 %collective-permute-start.18 = (bf16[128,768]{0,1:T(8,128)(2,1)S(1)}, bf16[128,768]{0,1:T(8,128)(2,1)S(1)}, u32[]{:S(2)}, u32[]{:S(2)}) collective-permute-start(bf16[128,768]{0,1:T(8,128)(2,1)S(1)} %get-tuple-element.14), channel_id=1, source_target_pairs={{0,8},{4,12},{8,0},{12,4},{16,24},{20,28},{24,16},{28,20},{1,9},{5... | collective-permute-start | bytes 589832 | tf_op jit(solution)/shard_map/ppermute | solution.py:17
  63.0 8.8 %collective-permute-start.16 = (bf16[128,768]{0,1:T(8,128)(2,1)S(1)}, bf16[128,768]{0,1:T(8,128)(2,1)S(1)}, u32[]{:S(2)}, u32[]{:S(2)}) collective-permute-start(bf16[128,768]{0,1:T(8,128)(2,1)S(1)} %get-tuple-element.14), channel_id=1, source_target_pairs={{0,4},{4,0},{8,12},{12,8},{16,20},{20,16},{24,28},{28,24},{1,5},{5... | collective-permute-start | bytes 589832 | tf_op jit(solution)/shard_map/ppermute | solution.py:17
  63.6 8.2 %collective-permute-start.19 = (bf16[128,768]{0,1:T(8,128)(2,1)S(1)}, bf16[128,768]{0,1:T(8,128)(2,1)S(1)}, u32[]{:S(2)}, u32[]{:S(2)}) collective-permute-start(bf16[128,768]{0,1:T(8,128)(2,1)S(1)} %convolution_convert_fusion.6), channel_id=1, source_target_pairs={{0,8},{4,12},{8,0},{12,4},{16,24},{20,28},{24,16},{28,20},{1,9},{5... | collective-permute-start | bytes 589832 | tf_op jit(solution)/shard_map/ppermute | solution.py:17
  72.8 7.0 %collective-permute-start.22 = (bf16[128,768]{0,1:T(8,128)(2,1)S(1)}, bf16[128,768]{0,1:T(8,128)(2,1)S(1)}, u32[]{:S(2)}, u32[]{:S(2)}) collective-permute-start(bf16[128,768]{0,1:T(8,128)(2,1)S(1)} %get-tuple-element.16), channel_id=1, source_target_pairs={{0,8},{4,12},{8,0},{12,4},{16,24},{20,28},{24,16},{28,20},{1,9},{5... | collective-permute-start | bytes 589832 | tf_op jit(solution)/shard_map/ppermute | solution.py:17
  74.1 8.7 %collective-permute-start.20 = (bf16[128,768]{0,1:T(8,128)(2,1)S(1)}, bf16[128,768]{0,1:T(8,128)(2,1)S(1)}, u32[]{:S(2)}, u32[]{:S(2)}) collective-permute-start(bf16[128,768]{0,1:T(8,128)(2,1)S(1)} %get-tuple-element.16), channel_id=1, source_target_pairs={{0,4},{4,0},{8,12},{12,8},{16,20},{20,16},{24,28},{28,24},{1,5},{5... | collective-permute-start | bytes 589832 | tf_op jit(solution)/shard_map/ppermute | solution.py:17
  74.6 8.1 %collective-permute-start.23 = (bf16[128,768]{0,1:T(8,128)(2,1)S(1)}, bf16[128,768]{0,1:T(8,128)(2,1)S(1)}, u32[]{:S(2)}, u32[]{:S(2)}) collective-permute-start(bf16[128,768]{0,1:T(8,128)(2,1)S(1)} %convolution_convert_fusion.4), channel_id=1, source_target_pairs={{0,8},{4,12},{8,0},{12,4},{16,24},{20,28},{24,16},{28,20},{1,9},{5... | collective-permute-start | bytes 589832 | tf_op jit(solution)/shard_map/ppermute | solution.py:17
  85.9 7.9 %collective-permute-start.24 = (bf16[128,768]{0,1:T(8,128)(2,1)S(1)}, bf16[128,768]{0,1:T(8,128)(2,1)S(1)}, u32[]{:S(2)}, u32[]{:S(2)}) collective-permute-start(bf16[128,768]{0,1:T(8,128)(2,1)S(1)} %get-tuple-element.18), channel_id=1, source_target_pairs={{0,4},{4,0},{8,12},{12,8},{16,20},{20,16},{24,28},{28,24},{1,5},{5... | collective-permute-start | bytes 589832 | tf_op jit(solution)/shard_map/ppermute | solution.py:17
  86.5 7.3 %collective-permute-start.27 = (bf16[128,768]{0,1:T(8,128)(2,1)S(1)}, bf16[128,768]{0,1:T(8,128)(2,1)S(1)}, u32[]{:S(2)}, u32[]{:S(2)}) collective-permute-start(bf16[128,768]{0,1:T(8,128)(2,1)S(1)} %convolution_convert_fusion.2), channel_id=1, source_target_pairs={{0,8},{4,12},{8,0},{12,4},{16,24},{20,28},{24,16},{28,20},{1,9},{5... | collective-permute-start | bytes 589832 | tf_op jit(solution)/shard_map/ppermute | solution.py:17
  95.5 7.9 %collective-permute-start.30 = (bf16[128,768]{0,1:T(8,128)(2,1)S(1)}, bf16[128,768]{0,1:T(8,128)(2,1)S(1)}, u32[]{:S(2)}, u32[]{:S(2)}) collective-permute-start(bf16[128,768]{0,1:T(8,128)(2,1)S(1)} %get-tuple-element.20), channel_id=1, source_target_pairs={{0,8},{4,12},{8,0},{12,4},{16,24},{20,28},{24,16},{28,20},{1,9},{5... | collective-permute-start | bytes 589832 | tf_op jit(solution)/shard_map/ppermute | solution.py:17
  97.1 9.2 %collective-permute-start.28 = (bf16[128,768]{0,1:T(8,128)(2,1)S(1)}, bf16[128,768]{0,1:T(8,128)(2,1)S(1)}, u32[]{:S(2)}, u32[]{:S(2)}) collective-permute-start(bf16[128,768]{0,1:T(8,128)(2,1)S(1)} %get-tuple-element.20), channel_id=1, source_target_pairs={{0,4},{4,0},{8,12},{12,8},{16,20},{20,16},{24,28},{28,24},{1,5},{5... | collective-permute-start | bytes 589832 | tf_op jit(solution)/shard_map/ppermute | solution.py:17
  97.1 6.8 %collective-permute-start.29 = (bf16[128,768]{0,1:T(8,128)(2,1)S(1)}, bf16[128,768]{0,1:T(8,128)(2,1)S(1)}, u32[]{:S(2)}, u32[]{:S(2)}) collective-permute-start(bf16[128,768]{0,1:T(8,128)(2,1)S(1)} %convolution_convert_fusion.1), channel_id=1, source_target_pairs={{0,4},{4,0},{8,12},{12,8},{16,20},{20,16},{24,28},{28,24},{1,5},{5... | collective-permute-start | bytes 589832 | tf_op jit(solution)/shard_map/ppermute | solution.py:17
  97.6 8.7 %collective-permute-start.31 = (bf16[128,768]{0,1:T(8,128)(2,1)S(1)}, bf16[128,768]{0,1:T(8,128)(2,1)S(1)}, u32[]{:S(2)}, u32[]{:S(2)}) collective-permute-start(bf16[128,768]{0,1:T(8,128)(2,1)S(1)} %convolution_convert_fusion), channel_id=1, source_target_pairs={{0,8},{4,12},{8,0},{12,4},{16,24},{20,28},{24,16},{28,20},{1,9},{5... | collective-permute-start | bytes 589832 | tf_op jit(solution)/shard_map/ppermute | solution.py:17
  (15 other events, 81.6 us)
